TPU v7x, 128 devices: a whole 4x4x4 slice. The times are simulated.
128 devices in a mesh: seq: 16 (over y, x), emb: 8 (over z, core).
Axes of the slice: x: 4, y: 4, z: 4, core: 2. Of those that a mesh axis runs over, the one named last changes fastest.
Arguments:
- source: bfloat16 [32768, 1024], P('seq', 'emb'), may hold values from -6 to 6
- target: bfloat16 [32768, 1024], P('seq', 'emb'), may hold values from -6 to 6
- doc_ids: int32 [32768], replicated, may hold values from 0 to 511, never falling along the last dimension, each value on 1 to 512 neighbouring positions
- offsets: int32 [512], P(('seq', 'emb')), may hold values from -2048 to 2048, as said below
Outputs:
- projected: bfloat16 [32768, 1024], P('seq', 'emb')
- row_mass: float32 [32768], P(('seq', 'emb'))
Inputs may be any that keep to these rules, and one draw needn't show every extreme that they name: doc_ids never fall along the sentences. `offsets`: both ends of the range occur in every draw.
All inputs are finite; a program needn't handle non-finite values.
Results may differ from a plain program's by a relative error of at most 0.006.
Values may be sent and summed in bfloat16 or wider, within the bound.
No kernel may reach another device: no remote copies, remote signals or barrier semaphores. Data moves between devices by JAX's collectives and lax.ppermute only.
A program may use at most 128 MiB of HBM per device.

v0:
```python
import jax
import jax.numpy as jnp
from jax import lax
from jax.sharding import PartitionSpec as P

BAND = 2048
OFFSET_BLOCK = 64
ITERS = 3
INV_EPS = 50.0
PENALTY = 0.04


def shifted_2(block, axis, distance):
    devices = range(lax.axis_size(axis))
    route = [(i - distance, i) for i in devices if i - distance in devices]
    return lax.ppermute(block, axis, route)


def per_device(source, target, doc_ids, offsets):
    n_emb = lax.axis_size("emb")
    rows_dev = source.shape[0] // n_emb
    place = lax.axis_index(("seq", "emb"))
    sentences = doc_ids.shape[0]
    reach = 2 * BAND
    hops = reach // rows_dev
    width = rows_dev + 2 * reach
    src_rows, tgt_rows = (
        lax.all_to_all(source, "emb", split_axis=0, concat_axis=1, tiled=True),
        lax.all_to_all(target, "emb", split_axis=0, concat_axis=1, tiled=True),
    )
    lower = {}
    upper = {}
    for dist in range(1, hops + 1):
        for sign in (1, -1):
            moved = shifted_2(tgt_rows, ("seq", "emb"), -sign * dist)
            if sign > 0:
                upper[dist] = moved
            else:
                lower[dist] = moved
    pieces = (
        [lower[dist] for dist in range(hops, 0, -1)]
        + [tgt_rows]
        + [upper[dist] for dist in range(1, hops + 1)]
    )
    window = jnp.concatenate(pieces, axis=0)
    src_scale = lax.rsqrt(jnp.sum(jnp.square(src_rows.astype(jnp.float32)), axis=1) + 1e-06)
    tgt_scale = lax.rsqrt(jnp.sum(jnp.square(window.astype(jnp.float32)), axis=1) + 1e-06)
    first_row = place * rows_dev
    src_pos = first_row + jnp.arange(rows_dev, dtype=jnp.int32)
    tgt_pos = first_row - reach + jnp.arange(width, dtype=jnp.int32)
    valid = (tgt_pos >= 0) & (tgt_pos < sentences)
    shifted = jnp.repeat(offsets, OFFSET_BLOCK)
    band = (jnp.abs(tgt_pos[None, :] - src_pos[:, None] - shifted[:, None]) <= BAND) & valid[
        None, :
    ]
    pad_docs = jnp.pad(doc_ids, (reach, reach), constant_values=-1)
    same = (
        lax.dynamic_slice_in_dim(doc_ids, first_row, rows_dev, 0)[:, None]
        == lax.dynamic_slice_in_dim(pad_docs, first_row, width, 0)[None, :]
    )
    penalty = jnp.where(same, 0.0, PENALTY)

    def cosines():
        dots = lax.dot_general(
            src_rows, window, (((1,), (1,)), ((), ())), preferred_element_type=jnp.float32
        )
        return dots * src_scale[:, None] * tgt_scale[None, :]

    def to_kernel(cosine):
        return jnp.where(band, jnp.exp((cosine - penalty) * INV_EPS), 0.0)

    def kernel():
        return to_kernel(cosines())

    padded_len = sentences + 2 * reach

    def column_scaling(part):
        full = lax.dynamic_update_slice_in_dim(
            jnp.zeros((padded_len,), jnp.float32), part, first_row, 0
        )
        columns = lax.psum(full, ("seq", "emb"))
        mine = lax.dynamic_slice_in_dim(columns, first_row, width, 0)
        return jnp.where(valid, 1.0 / jnp.where(valid, mine, 1.0), 0.0)

    scaling = valid.astype(jnp.float32)
    inverse = jnp.zeros((rows_dev,), jnp.float32)
    for step in range(ITERS):
        kern = kernel()
        inverse = 1.0 / jnp.sum(kern * scaling[None, :], axis=1)
        part = jnp.sum(kern * inverse[:, None], axis=0)
        scaling = column_scaling(part)
    kern = kernel()
    totals = jnp.sum(kern * scaling[None, :], axis=1)
    row_mass = inverse * totals
    weights = (kern * scaling[None, :] / totals[:, None]).astype(jnp.bfloat16)
    mixed = jnp.dot(weights, window, preferred_element_type=jnp.float32).astype(jnp.bfloat16)
    projected = lax.all_to_all(mixed, "emb", split_axis=1, concat_axis=0, tiled=True)
    return (projected, row_mass)


def solution(mesh):
    in_specs = (P("seq", "emb"), P("seq", "emb"), P(), P(("seq", "emb")))
    out_specs = (P("seq", "emb"), P(("seq", "emb")))
    return jax.shard_map(
        per_device, mesh=mesh, in_specs=in_specs, out_specs=out_specs, check_vma=False
    )
```

profile of v0, /device:TPU:1, one launch (start us, length us, event | category | flops | bytes accessed | tf_op | source)
XLA Modules:
  0.0 916.7 jit_solution(1106504656335570832)
XLA Ops:
  7.2 6.8 all-to-all-start
  14.0 9.3 %all-to-all-done = bf16[8,256,128]{2,1,0:T(8,128)(2,1)S(1)} async-done(((bf16[8,256,128]{2,1,0:T(8,128)(2,1)}), bf16[8,256,128]{2,1,0:T(8,128)(2,1)S(1)}, u32[]{:S(2)}, u32[]{:S(2)}) %all-to-all-start) | async-done | bytes 524320 | tf_op jit(solution)/shard_map/all_to_all | solution.py:29
  79.6 9.9 %collective-permute-done.4 = bf16[256,1024]{0,1:T(8,128)(2,1)S(1)} collective-permute-done((bf16[256,1024]{0,1:T(8,128)(2,1)S(1)}, bf16[256,1024]{0,1:T(8,128)(2,1)S(1)}, u32[]{:S(2)}, u32[]{:S(2)}) %collective-permute-start.4) | collective-permute-done | bytes 524320 | tf_op jit(solution)/shard_map/ppermute | solution.py:16
  89.5 11.1 %collective-permute-start.9 = (bf16[256,1024]{0,1:T(8,128)(2,1)S(1)}, bf16[256,1024]{0,1:T(8,128)(2,1)S(1)}, u32[]{:S(2)}, u32[]{:S(2)}) collective-permute-start(bf16[256,1024]{0,1:T(8,128)(2,1)S(1)} %bitcast.38), channel_id=1, source_target_pairs={{0,7},{1,8},{2,9},{3,10},{4,11},{5,12},{6,13},{7,14},{8,15},{9,16}... | collective-permute-start | bytes 1572872 | tf_op jit(solution)/shard_map/ppermute | solution.py:16
  105.1 6.9 collective-permute-done.6
  127.9 6.6 collective-permute-done.8
  141.1 7.7 collective-permute-start.14
  148.8 13.2 %collective-permute-start.15 = (bf16[256,1024]{0,1:T(8,128)(2,1)S(1)}, bf16[256,1024]{0,1:T(8,128)(2,1)S(1)}, u32[]{:S(2)}, u32[]{:S(2)}) collective-permute-start(bf16[256,1024]{0,1:T(8,128)(2,1)S(1)} %bitcast.44), channel_id=1, source_target_pairs={{0,1},{1,2},{2,3},{3,4},{4,5},{5,6},{6,7},{7,8},{8,9},{9,10},{10,1... | collective-permute-start | bytes 1572872 | tf_op jit(solution)/shard_map/ppermute | solution.py:16
  182.3 12.5 %collective-permute-done.18 = bf16[256,1024]{0,1:T(8,128)(2,1)S(1)} collective-permute-done((bf16[256,1024]{0,1:T(8,128)(2,1)S(1)}, bf16[256,1024]{0,1:T(8,128)(2,1)S(1)}, u32[]{:S(2)}, u32[]{:S(2)}) %collective-permute-start.18) | collective-permute-done | bytes 524320 | tf_op jit(solution)/shard_map/ppermute | solution.py:16
  196.2 9.9 %collective-permute-done.19 = bf16[256,1024]{0,1:T(8,128)(2,1)S(1)} collective-permute-done((bf16[256,1024]{0,1:T(8,128)(2,1)S(1)}, bf16[256,1024]{0,1:T(8,128)(2,1)S(1)}, u32[]{:S(2)}, u32[]{:S(2)}) %collective-permute-start.19) | collective-permute-done | bytes 524320 | tf_op jit(solution)/shard_map/ppermute | solution.py:16
  207.4 14.2 %collective-permute-done.20 = bf16[256,1024]{0,1:T(8,128)(2,1)S(1)} collective-permute-done((bf16[256,1024]{0,1:T(8,128)(2,1)S(1)}, bf16[256,1024]{0,1:T(8,128)(2,1)S(1)}, u32[]{:S(2)}, u32[]{:S(2)}) %collective-permute-start.20) | collective-permute-done | bytes 524320 | tf_op jit(solution)/shard_map/ppermute | solution.py:16
  222.9 9.9 %collective-permute-done.21 = bf16[256,1024]{0,1:T(8,128)(2,1)S(1)} collective-permute-done((bf16[256,1024]{0,1:T(8,128)(2,1)S(1)}, bf16[256,1024]{0,1:T(8,128)(2,1)S(1)}, u32[]{:S(2)}, u32[]{:S(2)}) %collective-permute-start.21) | collective-permute-done | bytes 524320 | tf_op jit(solution)/shard_map/ppermute | solution.py:16
  234.1 28.2 %collective-permute-done.22 = bf16[256,1024]{0,1:T(8,128)(2,1)S(1)} collective-permute-done((bf16[256,1024]{0,1:T(8,128)(2,1)S(1)}, bf16[256,1024]{0,1:T(8,128)(2,1)S(1)}, u32[]{:S(2)}, u32[]{:S(2)}) %collective-permute-start.22) | collective-permute-done | bytes 524320 | tf_op jit(solution)/shard_map/ppermute | solution.py:16
  266.6 26.9 %collective-permute-done.24 = bf16[256,1024]{0,1:T(8,128)(2,1)S(1)} collective-permute-done((bf16[256,1024]{0,1:T(8,128)(2,1)S(1)}, bf16[256,1024]{0,1:T(8,128)(2,1)S(1)}, u32[]{:S(2)}, u32[]{:S(2)}) %collective-permute-start.24) | collective-permute-done | bytes 524320 | tf_op jit(solution)/shard_map/ppermute | solution.py:16
  300.3 8.9 collective-permute-done.26
  310.6 15.1 %collective-permute-done.27 = bf16[256,1024]{0,1:T(8,128)(2,1)S(1)} collective-permute-done((bf16[256,1024]{0,1:T(8,128)(2,1)S(1)}, bf16[256,1024]{0,1:T(8,128)(2,1)S(1)}, u32[]{:S(2)}, u32[]{:S(2)}) %collective-permute-start.27) | collective-permute-done | bytes 524320 | tf_op jit(solution)/shard_map/ppermute | solution.py:16
  325.7 8.9 collective-permute-done.28
  338.7 35.5 %collective-permute-done.30 = bf16[256,1024]{0,1:T(8,128)(2,1)S(1)} collective-permute-done((bf16[256,1024]{0,1:T(8,128)(2,1)S(1)}, bf16[256,1024]{0,1:T(8,128)(2,1)S(1)}, u32[]{:S(2)}, u32[]{:S(2)}) %collective-permute-start.30) | collective-permute-done | bytes 524320 | tf_op jit(solution)/shard_map/ppermute | solution.py:16
  378.6 11.5 %multiply_reduce_fusion.6 = (f32[256]{0:T(256)S(1)}, f32[256,8448]{0,1:T(8,128)S(1)}) fusion(f32[8448]{0:T(1024)S(1)} %get-tuple-element.5, s32[8448]{0:T(1024)S(1)} %get-tuple-element.6, s32[256]{0:T(256)S(1)} %dynamic_slice.15, f32[8448]{0:T(1024)S(1)} %add_rsqrt_fusion, f32[256]{0:T(256)S(1)} %add_rsqrt_fusion.1, ...), kind=kOutput, calls=%fused_computation.14 | convolution fusion | flops 4459462656 | bytes 26625280 | tf_op jit(solution)/shard_map/dot_general | solution.py:64
  396.2 171.8 %all-reduce.5.cloned.1.call-done = f32[40960]{0:T(1024)} async-done(((f32[40960]{0:T(1024)}), f32[40960]{0:T(1024)}) %all-reduce.5.cloned.1.call-update) | async-done | bytes 163856 | tf_op jit(solution)/shard_map/psum | solution.py:81
  580.2 141.7 %all-reduce.7.cloned.1.call-done = f32[40960]{0:T(1024)} async-done(((f32[40960]{0:T(1024)}), f32[40960]{0:T(1024)}) %all-reduce.7.cloned.1.call-update) | async-done | bytes 163856 | tf_op jit(solution)/shard_map/psum | solution.py:81
  734.0 141.8 %all-reduce.9.cloned.1.call-done = f32[40960]{0:T(1024)} async-done(((f32[40960]{0:T(1024)}), f32[40960]{0:T(1024)}) %all-reduce.9.cloned.1.call-update) | async-done | bytes 163856 | tf_op jit(solution)/shard_map/psum | solution.py:81
  882.4 12.8 %fusion.11 = bf16[32,8,8,128]{3,2,1,0:T(8,128)(2,1)S(1)} fusion(bf16[8448,1024]{0,1:T(8,128)(2,1)} %copy-done.1, f32[256,8448]{0,1:T(8,128)} %copy-done, f32[256]{0:T(256)S(1)} %multiply_reduce_fusion.7, f32[8448]{0:T(1024)S(1)} %divide_select_fusion), kind=kOutput, calls=%fused_computation.22 | convolution fusion | flops 4435935232 | bytes 26511360 | tf_op jit(solution)/shard_map/dot_general | solution.py:96
  900.6 8.8 all-to-all-done.2
  (133 shorter events, 172.4 us)
Async XLA Ops:
  27.7 540.3 %all-reduce.5.cloned.1.call-start = ((), (), s32[]{:S(2)}) async-start(), calls=%async_computation.3 | async-start | bytes 327680 | tf_op jit(solution)/shard_map/psum | solution.py:81
  48.3 41.3 %collective-permute-start.4 = (bf16[256,1024]{0,1:T(8,128)(2,1)S(1)}, bf16[256,1024]{0,1:T(8,128)(2,1)S(1)}, u32[]{:S(2)}, u32[]{:S(2)}) collective-permute-start(bf16[256,1024]{0,1:T(8,128)(2,1)S(1)} %bitcast.33), channel_id=1, source_target_pairs={{0,12},{1,13},{2,14},{3,15},{4,16},{5,17},{6,18},{7,19},{8,20},{9,... | collective-permute-start | bytes 1572872 | tf_op jit(solution)/shard_map/ppermute | solution.py:16
  53.4 47.4 %collective-permute-start.5 = (bf16[256,1024]{0,1:T(8,128)(2,1)S(1)}, bf16[256,1024]{0,1:T(8,128)(2,1)S(1)}, u32[]{:S(2)}, u32[]{:S(2)}) collective-permute-start(bf16[256,1024]{0,1:T(8,128)(2,1)S(1)} %bitcast.34), channel_id=1, source_target_pairs={{0,11},{1,12},{2,13},{3,14},{4,15},{5,16},{6,17},{7,18},{8,19},{9,... | collective-permute-start | bytes 1572872 | tf_op jit(solution)/shard_map/ppermute | solution.py:16
  60.5 51.5 %collective-permute-start.6 = (bf16[256,1024]{0,1:T(8,128)(2,1)S(1)}, bf16[256,1024]{0,1:T(8,128)(2,1)S(1)}, u32[]{:S(2)}, u32[]{:S(2)}) collective-permute-start(bf16[256,1024]{0,1:T(8,128)(2,1)S(1)} %bitcast.35), channel_id=1, source_target_pairs={{0,10},{1,11},{2,12},{3,13},{4,14},{5,15},{6,16},{7,17},{8,18},{9,... | collective-permute-start | bytes 1572872 | tf_op jit(solution)/shard_map/ppermute | solution.py:16
  67.1 56.2 %collective-permute-start.7 = (bf16[256,1024]{0,1:T(8,128)(2,1)S(1)}, bf16[256,1024]{0,1:T(8,128)(2,1)S(1)}, u32[]{:S(2)}, u32[]{:S(2)}) collective-permute-start(bf16[256,1024]{0,1:T(8,128)(2,1)S(1)} %bitcast.36), channel_id=1, source_target_pairs={{0,9},{1,10},{2,11},{3,12},{4,13},{5,14},{6,15},{7,16},{8,17},{9,1... | collective-permute-start | bytes 1572872 | tf_op jit(solution)/shard_map/ppermute | solution.py:16
  78.3 56.2 %collective-permute-start.8 = (bf16[256,1024]{0,1:T(8,128)(2,1)S(1)}, bf16[256,1024]{0,1:T(8,128)(2,1)S(1)}, u32[]{:S(2)}, u32[]{:S(2)}) collective-permute-start(bf16[256,1024]{0,1:T(8,128)(2,1)S(1)} %bitcast.37), channel_id=1, source_target_pairs={{0,8},{1,9},{2,10},{3,11},{4,12},{5,13},{6,14},{7,15},{8,16},{9,17... | collective-permute-start | bytes 1572872 | tf_op jit(solution)/shard_map/ppermute | solution.py:16
  89.5 51.6 %collective-permute-start.9 = (bf16[256,1024]{0,1:T(8,128)(2,1)S(1)}, bf16[256,1024]{0,1:T(8,128)(2,1)S(1)}, u32[]{:S(2)}, u32[]{:S(2)}) collective-permute-start(bf16[256,1024]{0,1:T(8,128)(2,1)S(1)} %bitcast.38), channel_id=1, source_target_pairs={{0,7},{1,8},{2,9},{3,10},{4,11},{5,12},{6,13},{7,14},{8,15},{9,16}... | collective-permute-start | bytes 1572872 | tf_op jit(solution)/shard_map/ppermute | solution.py:16
  100.8 48.1 %collective-permute-start.10 = (bf16[256,1024]{0,1:T(8,128)(2,1)S(1)}, bf16[256,1024]{0,1:T(8,128)(2,1)S(1)}, u32[]{:S(2)}, u32[]{:S(2)}) collective-permute-start(bf16[256,1024]{0,1:T(8,128)(2,1)S(1)} %bitcast.39), channel_id=1, source_target_pairs={{0,6},{1,7},{2,8},{3,9},{4,10},{5,11},{6,12},{7,13},{8,14},{9,15},... | collective-permute-start | bytes 1572872 | tf_op jit(solution)/shard_map/ppermute | solution.py:16
  112.0 50.1 %collective-permute-start.11 = (bf16[256,1024]{0,1:T(8,128)(2,1)S(1)}, bf16[256,1024]{0,1:T(8,128)(2,1)S(1)}, u32[]{:S(2)}, u32[]{:S(2)}) collective-permute-start(bf16[256,1024]{0,1:T(8,128)(2,1)S(1)} %bitcast.40), channel_id=1, source_target_pairs={{0,5},{1,6},{2,7},{3,8},{4,9},{5,10},{6,11},{7,12},{8,13},{9,14},{... | collective-permute-start | bytes 1572872 | tf_op jit(solution)/shard_map/ppermute | solution.py:16
  123.2 40.8 %collective-permute-start.12 = (bf16[256,1024]{0,1:T(8,128)(2,1)S(1)}, bf16[256,1024]{0,1:T(8,128)(2,1)S(1)}, u32[]{:S(2)}, u32[]{:S(2)}) collective-permute-start(bf16[256,1024]{0,1:T(8,128)(2,1)S(1)} %bitcast.41), channel_id=1, source_target_pairs={{0,4},{1,5},{2,6},{3,7},{4,8},{5,9},{6,10},{7,11},{8,12},{9,13},{1... | collective-permute-start | bytes 1572872 | tf_op jit(solution)/shard_map/ppermute | solution.py:16
  168.1 53.4 %collective-permute-start.20 = (bf16[256,1024]{0,1:T(8,128)(2,1)S(1)}, bf16[256,1024]{0,1:T(8,128)(2,1)S(1)}, u32[]{:S(2)}, u32[]{:S(2)}) collective-permute-start(bf16[256,1024]{0,1:T(8,128)(2,1)S(1)} %bitcast.49), channel_id=1, source_target_pairs={{5,0},{6,1},{7,2},{8,3},{9,4},{10,5},{11,6},{12,7},{13,8},{14,9},{... | collective-permute-start | bytes 1572872 | tf_op jit(solution)/shard_map/ppermute | solution.py:16
  175.7 57.1 %collective-permute-start.21 = (bf16[256,1024]{0,1:T(8,128)(2,1)S(1)}, bf16[256,1024]{0,1:T(8,128)(2,1)S(1)}, u32[]{:S(2)}, u32[]{:S(2)}) collective-permute-start(bf16[256,1024]{0,1:T(8,128)(2,1)S(1)} %bitcast.51), channel_id=1, source_target_pairs={{6,0},{7,1},{8,2},{9,3},{10,4},{11,5},{12,6},{13,7},{14,8},{15,9},... | collective-permute-start | bytes 1572872 | tf_op jit(solution)/shard_map/ppermute | solution.py:16
  180.9 81.3 %collective-permute-start.22 = (bf16[256,1024]{0,1:T(8,128)(2,1)S(1)}, bf16[256,1024]{0,1:T(8,128)(2,1)S(1)}, u32[]{:S(2)}, u32[]{:S(2)}) collective-permute-start(bf16[256,1024]{0,1:T(8,128)(2,1)S(1)} %bitcast.52), channel_id=1, source_target_pairs={{7,0},{8,1},{9,2},{10,3},{11,4},{12,5},{13,6},{14,7},{15,8},{16,9}... | collective-permute-start | bytes 1572872 | tf_op jit(solution)/shard_map/ppermute | solution.py:16
  194.8 70.5 %collective-permute-start.23 = (bf16[256,1024]{0,1:T(8,128)(2,1)S(1)}, bf16[256,1024]{0,1:T(8,128)(2,1)S(1)}, u32[]{:S(2)}, u32[]{:S(2)}) collective-permute-start(bf16[256,1024]{0,1:T(8,128)(2,1)S(1)} %bitcast.53), channel_id=1, source_target_pairs={{8,0},{9,1},{10,2},{11,3},{12,4},{13,5},{14,6},{15,7},{16,8},{17,9... | collective-permute-start | bytes 1572872 | tf_op jit(solution)/shard_map/ppermute | solution.py:16
  206.1 87.5 %collective-permute-start.24 = (bf16[256,1024]{0,1:T(8,128)(2,1)S(1)}, bf16[256,1024]{0,1:T(8,128)(2,1)S(1)}, u32[]{:S(2)}, u32[]{:S(2)}) collective-permute-start(bf16[256,1024]{0,1:T(8,128)(2,1)S(1)} %bitcast.54), channel_id=1, source_target_pairs={{9,0},{10,1},{11,2},{12,3},{13,4},{14,5},{15,6},{16,7},{17,8},{18,... | collective-permute-start | bytes 1572872 | tf_op jit(solution)/shard_map/ppermute | solution.py:16
  221.5 77.4 %collective-permute-start.25 = (bf16[256,1024]{0,1:T(8,128)(2,1)S(1)}, bf16[256,1024]{0,1:T(8,128)(2,1)S(1)}, u32[]{:S(2)}, u32[]{:S(2)}) collective-permute-start(bf16[256,1024]{0,1:T(8,128)(2,1)S(1)} %bitcast.55), channel_id=1, source_target_pairs={{10,0},{11,1},{12,2},{13,3},{14,4},{15,5},{16,6},{17,7},{18,8},{19... | collective-permute-start | bytes 1572872 | tf_op jit(solution)/shard_map/ppermute | solution.py:16
  232.8 76.5 %collective-permute-start.26 = (bf16[256,1024]{0,1:T(8,128)(2,1)S(1)}, bf16[256,1024]{0,1:T(8,128)(2,1)S(1)}, u32[]{:S(2)}, u32[]{:S(2)}) collective-permute-start(bf16[256,1024]{0,1:T(8,128)(2,1)S(1)} %bitcast.56), channel_id=1, source_target_pairs={{11,0},{12,1},{13,2},{14,3},{15,4},{16,5},{17,6},{18,7},{19,8},{20... | collective-permute-start | bytes 1572872 | tf_op jit(solution)/shard_map/ppermute | solution.py:16
  262.3 63.4 %collective-permute-start.27 = (bf16[256,1024]{0,1:T(8,128)(2,1)S(1)}, bf16[256,1024]{0,1:T(8,128)(2,1)S(1)}, u32[]{:S(2)}, u32[]{:S(2)}) collective-permute-start(bf16[256,1024]{0,1:T(8,128)(2,1)S(1)} %bitcast.57), channel_id=1, source_target_pairs={{12,0},{13,1},{14,2},{15,3},{16,4},{17,5},{18,6},{19,7},{20,8},{21... | collective-permute-start | bytes 1572872 | tf_op jit(solution)/shard_map/ppermute | solution.py:16
  265.3 69.4 %collective-permute-start.28 = (bf16[256,1024]{0,1:T(8,128)(2,1)S(1)}, bf16[256,1024]{0,1:T(8,128)(2,1)S(1)}, u32[]{:S(2)}, u32[]{:S(2)}) collective-permute-start(bf16[256,1024]{0,1:T(8,128)(2,1)S(1)} %bitcast.58), channel_id=1, source_target_pairs={{13,0},{14,1},{15,2},{16,3},{17,4},{18,5},{19,6},{20,7},{21,8},{22... | collective-permute-start | bytes 1572872 | tf_op jit(solution)/shard_map/ppermute | solution.py:16
  293.5 45.1 %collective-permute-start.29 = (bf16[256,1024]{0,1:T(8,128)(2,1)S(1)}, bf16[256,1024]{0,1:T(8,128)(2,1)S(1)}, u32[]{:S(2)}, u32[]{:S(2)}) collective-permute-start(bf16[256,1024]{0,1:T(8,128)(2,1)S(1)} %bitcast.59), channel_id=1, source_target_pairs={{14,0},{15,1},{16,2},{17,3},{18,4},{19,5},{20,6},{21,7},{22,8},{23... | collective-permute-start | bytes 1572872 | tf_op jit(solution)/shard_map/ppermute | solution.py:16
  299.0 75.2 %collective-permute-start.30 = (bf16[256,1024]{0,1:T(8,128)(2,1)S(1)}, bf16[256,1024]{0,1:T(8,128)(2,1)S(1)}, u32[]{:S(2)}, u32[]{:S(2)}) collective-permute-start(bf16[256,1024]{0,1:T(8,128)(2,1)S(1)} %bitcast.60), channel_id=1, source_target_pairs={{15,0},{16,1},{17,2},{18,3},{19,4},{20,5},{21,6},{22,7},{23,8},{24... | collective-permute-start | bytes 1572872 | tf_op jit(solution)/shard_map/ppermute | solution.py:16
  309.3 65.4 %collective-permute-start.31 = (bf16[256,1024]{0,1:T(8,128)(2,1)S(1)}, bf16[256,1024]{0,1:T(8,128)(2,1)S(1)}, u32[]{:S(2)}, u32[]{:S(2)}) collective-permute-start(bf16[256,1024]{0,1:T(8,128)(2,1)S(1)} %bitcast.61), channel_id=1, source_target_pairs={{16,0},{17,1},{18,2},{19,3},{20,4},{21,5},{22,6},{23,7},{24,8},{25... | collective-permute-start | bytes 1572872 | tf_op jit(solution)/shard_map/ppermute | solution.py:16
  396.2 325.8 %all-reduce.7.cloned.1.call-start = ((), (), s32[]{:S(2)}) async-start(), calls=%async_computation.4 | async-start | bytes 327680 | tf_op jit(solution)/shard_map/psum | solution.py:81
  580.1 295.7 %all-reduce.9.cloned.1.call-start = ((), (), s32[]{:S(2)}) async-start(), calls=%async_computation.5 | async-start | bytes 327680 | tf_op jit(solution)/shard_map/psum | solution.py:81
  (19 other events, 367.7 us)
Sparse Core Ops, SparseCore 0:
  396.3 171.6 all-reduce.4
  580.2 141.6 all-reduce.6
  734.2 141.6 all-reduce.8
where the time goes:
time: 918 us; the launch traced here: 917 us
  waiting for transfers between devices  702 us (76%)
  starting transfers between devices  127 us (14%)
  other arithmetic  35.1 us (4%)
  matrix products  24.3 us (3%)
  between operations  14.5 us (2%)
  local copies, waits for them, and re-layouts  14.1 us (2%)
    psum x3, waiting for transfers between devices, column_scaling(): columns = lax.psum(full, ('seq', 'emb'))  455 us
    ppermute x32, waiting for transfers between devices, shifted_2(): return lax.ppermute(block, axis, route)  228 us
    ppermute x32, starting transfers between devices, shifted_2(): return lax.ppermute(block, axis, route)  112 us
  transfers between devices with their start and end apart: 38, of which 28 were waited for; matrix products, arithmetic and copies ran while one was open for 1% of the time, Pallas kernels for 0%

commit v1 on v0

--- a/solution.py
+++ b/solution.py
@@ -78,7 +78,7 @@
         full = lax.dynamic_update_slice_in_dim(
             jnp.zeros((padded_len,), jnp.float32), part, first_row, 0
         )
-        columns = lax.psum(full, ("seq", "emb"))
+        columns = jnp.sum(lax.all_gather(full, ("seq", "emb")), axis=0)
         mine = lax.dynamic_slice_in_dim(columns, first_row, width, 0)
         return jnp.where(valid, 1.0 / jnp.where(valid, mine, 1.0), 0.0)
 

time: 918 us -> 792 us (0.86)
  waiting for transfers between devices: 702 us -> 534 us
  other arithmetic: 35.1 us -> 78.7 us
    psum x3 -> x0, waiting for transfers between devices: 455 us -> none  [column_scaling(): columns = lax.psum(full, ('seq', 'emb'))]
    all_gather x0 -> x3, waiting for transfers between devices: none -> 288 us  [column_scaling(): columns = jnp.sum(lax.all_gather(full, ('seq', 'emb')), axis=0)]
    reduce_sum x0 -> x3, other arithmetic: none -> 45.9 us  [column_scaling(): columns = jnp.sum(lax.all_gather(full, ('seq', 'emb')), axis=0)]
where the time goes in v1:
time: 792 us; the launch traced here: 791 us
  waiting for transfers between devices  534 us (67%)
  starting transfers between devices  127 us (16%)
  other arithmetic  78.7 us (10%)
  matrix products  24.2 us (3%)
  between operations  14.5 us (2%)
  local copies, waits for them, and re-layouts  12.7 us (2%)
    all_gather x3, waiting for transfers between devices, column_scaling(): columns = jnp.sum(lax.all_gather(full, ('seq', 'emb')), axis=0)  288 us
    ppermute x32, waiting for transfers between devices, shifted_2(): return lax.ppermute(block, axis, route)  228 us
    ppermute x32, starting transfers between devices, shifted_2(): return lax.ppermute(block, axis, route)  112 us
    reduce_sum x3, other arithmetic, column_scaling(): columns = jnp.sum(lax.all_gather(full, ('seq', 'emb')), axis=0)  45.9 us
  transfers between devices with their start and end apart: 38, of which 28 were waited for; matrix products, arithmetic and copies ran while one was open for 1% of the time, Pallas kernels for 0%

profile of v1, /device:TPU:1, one launch (start us, length us, event | category | flops | bytes accessed | tf_op | source)
XLA Modules:
  0.0 790.9 jit_solution(408196945838685765)
XLA Ops:
  14.0 9.3 %all-to-all-done = bf16[8,256,128]{2,1,0:T(8,128)(2,1)S(1)} async-done(((bf16[8,256,128]{2,1,0:T(8,128)(2,1)}), bf16[8,256,128]{2,1,0:T(8,128)(2,1)S(1)}, u32[]{:S(2)}, u32[]{:S(2)}) %all-to-all-start) | async-done | bytes 524320 | tf_op jit(solution)/shard_map/all_to_all | solution.py:29
  79.6 9.9 %collective-permute-done.4 = bf16[256,1024]{0,1:T(8,128)(2,1)S(1)} collective-permute-done((bf16[256,1024]{0,1:T(8,128)(2,1)S(1)}, bf16[256,1024]{0,1:T(8,128)(2,1)S(1)}, u32[]{:S(2)}, u32[]{:S(2)}) %collective-permute-start.4) | collective-permute-done | bytes 524320 | tf_op jit(solution)/shard_map/ppermute | solution.py:16
  89.5 11.1 %collective-permute-start.9 = (bf16[256,1024]{0,1:T(8,128)(2,1)S(1)}, bf16[256,1024]{0,1:T(8,128)(2,1)S(1)}, u32[]{:S(2)}, u32[]{:S(2)}) collective-permute-start(bf16[256,1024]{0,1:T(8,128)(2,1)S(1)} %bitcast.38), channel_id=1, source_target_pairs={{0,7},{1,8},{2,9},{3,10},{4,11},{5,12},{6,13},{7,14},{8,15},{9,16}... | collective-permute-start | bytes 1572872 | tf_op jit(solution)/shard_map/ppermute | solution.py:16
  141.1 7.7 collective-permute-start.14
  148.8 13.2 %collective-permute-start.15 = (bf16[256,1024]{0,1:T(8,128)(2,1)S(1)}, bf16[256,1024]{0,1:T(8,128)(2,1)S(1)}, u32[]{:S(2)}, u32[]{:S(2)}) collective-permute-start(bf16[256,1024]{0,1:T(8,128)(2,1)S(1)} %bitcast.44), channel_id=1, source_target_pairs={{0,1},{1,2},{2,3},{3,4},{4,5},{5,6},{6,7},{7,8},{8,9},{9,10},{10,1... | collective-permute-start | bytes 1572872 | tf_op jit(solution)/shard_map/ppermute | solution.py:16
  182.3 12.5 %collective-permute-done.18 = bf16[256,1024]{0,1:T(8,128)(2,1)S(1)} collective-permute-done((bf16[256,1024]{0,1:T(8,128)(2,1)S(1)}, bf16[256,1024]{0,1:T(8,128)(2,1)S(1)}, u32[]{:S(2)}, u32[]{:S(2)}) %collective-permute-start.18) | collective-permute-done | bytes 524320 | tf_op jit(solution)/shard_map/ppermute | solution.py:16
  196.2 9.9 %collective-permute-done.19 = bf16[256,1024]{0,1:T(8,128)(2,1)S(1)} collective-permute-done((bf16[256,1024]{0,1:T(8,128)(2,1)S(1)}, bf16[256,1024]{0,1:T(8,128)(2,1)S(1)}, u32[]{:S(2)}, u32[]{:S(2)}) %collective-permute-start.19) | collective-permute-done | bytes 524320 | tf_op jit(solution)/shard_map/ppermute | solution.py:16
  207.4 14.2 %collective-permute-done.20 = bf16[256,1024]{0,1:T(8,128)(2,1)S(1)} collective-permute-done((bf16[256,1024]{0,1:T(8,128)(2,1)S(1)}, bf16[256,1024]{0,1:T(8,128)(2,1)S(1)}, u32[]{:S(2)}, u32[]{:S(2)}) %collective-permute-start.20) | collective-permute-done | bytes 524320 | tf_op jit(solution)/shard_map/ppermute | solution.py:16
  222.9 9.9 %collective-permute-done.21 = bf16[256,1024]{0,1:T(8,128)(2,1)S(1)} collective-permute-done((bf16[256,1024]{0,1:T(8,128)(2,1)S(1)}, bf16[256,1024]{0,1:T(8,128)(2,1)S(1)}, u32[]{:S(2)}, u32[]{:S(2)}) %collective-permute-start.21) | collective-permute-done | bytes 524320 | tf_op jit(solution)/shard_map/ppermute | solution.py:16
  234.1 28.2 %collective-permute-done.22 = bf16[256,1024]{0,1:T(8,128)(2,1)S(1)} collective-permute-done((bf16[256,1024]{0,1:T(8,128)(2,1)S(1)}, bf16[256,1024]{0,1:T(8,128)(2,1)S(1)}, u32[]{:S(2)}, u32[]{:S(2)}) %collective-permute-start.22) | collective-permute-done | bytes 524320 | tf_op jit(solution)/shard_map/ppermute | solution.py:16
  266.6 26.9 %collective-permute-done.24 = bf16[256,1024]{0,1:T(8,128)(2,1)S(1)} collective-permute-done((bf16[256,1024]{0,1:T(8,128)(2,1)S(1)}, bf16[256,1024]{0,1:T(8,128)(2,1)S(1)}, u32[]{:S(2)}, u32[]{:S(2)}) %collective-permute-start.24) | collective-permute-done | bytes 524320 | tf_op jit(solution)/shard_map/ppermute | solution.py:16
  300.3 8.9 %collective-permute-done.26 = bf16[256,1024]{0,1:T(8,128)(2,1)S(1)} collective-permute-done((bf16[256,1024]{0,1:T(8,128)(2,1)S(1)}, bf16[256,1024]{0,1:T(8,128)(2,1)S(1)}, u32[]{:S(2)}, u32[]{:S(2)}) %collective-permute-start.26) | collective-permute-done | bytes 524320 | tf_op jit(solution)/shard_map/ppermute | solution.py:16
  310.6 15.1 %collective-permute-done.27 = bf16[256,1024]{0,1:T(8,128)(2,1)S(1)} collective-permute-done((bf16[256,1024]{0,1:T(8,128)(2,1)S(1)}, bf16[256,1024]{0,1:T(8,128)(2,1)S(1)}, u32[]{:S(2)}, u32[]{:S(2)}) %collective-permute-start.27) | collective-permute-done | bytes 524320 | tf_op jit(solution)/shard_map/ppermute | solution.py:16
  325.7 8.9 %collective-permute-done.28 = bf16[256,1024]{0,1:T(8,128)(2,1)S(1)} collective-permute-done((bf16[256,1024]{0,1:T(8,128)(2,1)S(1)}, bf16[256,1024]{0,1:T(8,128)(2,1)S(1)}, u32[]{:S(2)}, u32[]{:S(2)}) %collective-permute-start.28) | collective-permute-done | bytes 524320 | tf_op jit(solution)/shard_map/ppermute | solution.py:16
  338.7 35.5 %collective-permute-done.30 = bf16[256,1024]{0,1:T(8,128)(2,1)S(1)} collective-permute-done((bf16[256,1024]{0,1:T(8,128)(2,1)S(1)}, bf16[256,1024]{0,1:T(8,128)(2,1)S(1)}, u32[]{:S(2)}, u32[]{:S(2)}) %collective-permute-start.30) | collective-permute-done | bytes 524320 | tf_op jit(solution)/shard_map/ppermute | solution.py:16
  378.6 11.5 %multiply_reduce_fusion.6 = (f32[256]{0:T(256)S(1)}, f32[256,8448]{0,1:T(8,128)S(1)}) fusion(f32[8448]{0:T(1024)S(1)} %get-tuple-element.5, s32[8448]{0:T(1024)S(1)} %get-tuple-element.6, s32[256]{0:T(256)S(1)} %dynamic_slice.15, f32[8448]{0:T(1024)S(1)} %add_rsqrt_fusion, f32[256]{0:T(256)S(1)} %add_rsqrt_fusion.1, ...), kind=kOutput, calls=%fused_computation.14 | convolution fusion | flops 4459462656 | bytes 26625280 | tf_op jit(solution)/shard_map/dot_general | solution.py:64
  395.7 115.1 %all-gather.7.cloned.1.call-done = f32[128,1,40960]{2,1,0:T(1,128)} async-done(((f32[1,1,40960]{2,1,0:T(1,128)}), f32[128,1,40960]{2,1,0:T(1,128)}) %all-gather.7.cloned.1.call-update) | async-done | bytes 20971536 | tf_op jit(solution)/shard_map/all_gather | solution.py:81
  510.8 15.3 %reduce_sum.112 = f32[40960]{0:T(1024)S(1)} reduce(f32[128,1,40960]{2,1,0:T(1,128)} %all-gather.7.cloned.1.call-done, f32[]{:T(128)} %constant.10.clone.1), dimensions={0,1}, to_apply=%region_4.5 | reduce | flops 5201920 | bytes 21135364 | tf_op jit(solution)/shard_map/reduce_sum | solution.py:81
  537.1 86.2 %all-gather.9.cloned.1.call-done = f32[128,1,40960]{2,1,0:T(1,128)} async-done(((f32[1,1,40960]{2,1,0:T(1,128)}), f32[128,1,40960]{2,1,0:T(1,128)}) %all-gather.9.cloned.1.call-update) | async-done | bytes 20971536 | tf_op jit(solution)/shard_map/all_gather | solution.py:81
  623.3 15.3 %reduce_sum.115 = f32[40960]{0:T(1024)S(1)} reduce(f32[128,1,40960]{2,1,0:T(1,128)} %all-gather.9.cloned.1.call-done, f32[]{:T(128)} %constant.10.clone.1), dimensions={0,1}, to_apply=%region_7.8 | reduce | flops 5201920 | bytes 21135364 | tf_op jit(solution)/shard_map/reduce_sum | solution.py:81
  649.4 86.3 %all-gather.11.cloned.1.call-done = f32[128,1,40960]{2,1,0:T(1,128)} async-done(((f32[1,1,40960]{2,1,0:T(1,128)}), f32[128,1,40960]{2,1,0:T(1,128)}) %all-gather.11.cloned.1.call-update) | async-done | bytes 20971536 | tf_op jit(solution)/shard_map/all_gather | solution.py:81
  735.7 15.3 %reduce_sum.118 = f32[40960]{0:T(1024)S(1)} reduce(f32[128,1,40960]{2,1,0:T(1,128)} %all-gather.11.cloned.1.call-done, f32[]{:T(128)} %constant.10.clone.1), dimensions={0,1}, to_apply=%region_10.11 | reduce | flops 5201920 | bytes 21135364 | tf_op jit(solution)/shard_map/reduce_sum | solution.py:81
  756.8 12.8 %fusion.11 = bf16[32,8,8,128]{3,2,1,0:T(8,128)(2,1)S(1)} fusion(bf16[8448,1024]{0,1:T(8,128)(2,1)} %copy-done.1, f32[256,8448]{0,1:T(8,128)} %copy-done, f32[256]{0:T(256)S(1)} %multiply_reduce_fusion.7, f32[8448]{0:T(1024)S(1)} %divide_select_fusion), kind=kOutput, calls=%fused_computation.22 | convolution fusion | flops 4435935232 | bytes 26511360 | tf_op jit(solution)/shard_map/dot_general | solution.py:96
  774.7 8.8 %all-to-all-done.2 = bf16[256,8,128]{2,0,1:T(8,128)(2,1)S(1)} async-done(((bf16[256,8,128]{2,0,1:T(8,128)(2,1)}), bf16[256,8,128]{2,0,1:T(8,128)(2,1)S(1)}, u32[]{:S(2)}, u32[]{:S(2)}) %all-to-all-start.2) | async-done | bytes 524320 | tf_op jit(solution)/shard_map/all_to_all | solution.py:97
  (136 shorter events, 188.6 us)
Async XLA Ops:
  27.7 483.1 %all-gather.7.cloned.1.call-start = ((), (), s32[]{:S(2)}) async-start(), calls=%async_computation.3 | async-start | bytes 21135360 | tf_op jit(solution)/shard_map/all_gather | solution.py:81
  48.3 41.3 %collective-permute-start.4 = (bf16[256,1024]{0,1:T(8,128)(2,1)S(1)}, bf16[256,1024]{0,1:T(8,128)(2,1)S(1)}, u32[]{:S(2)}, u32[]{:S(2)}) collective-permute-start(bf16[256,1024]{0,1:T(8,128)(2,1)S(1)} %bitcast.33), channel_id=1, source_target_pairs={{0,12},{1,13},{2,14},{3,15},{4,16},{5,17},{6,18},{7,19},{8,20},{9,... | collective-permute-start | bytes 1572872 | tf_op jit(solution)/shard_map/ppermute | solution.py:16
  53.4 47.4 %collective-permute-start.5 = (bf16[256,1024]{0,1:T(8,128)(2,1)S(1)}, bf16[256,1024]{0,1:T(8,128)(2,1)S(1)}, u32[]{:S(2)}, u32[]{:S(2)}) collective-permute-start(bf16[256,1024]{0,1:T(8,128)(2,1)S(1)} %bitcast.34), channel_id=1, source_target_pairs={{0,11},{1,12},{2,13},{3,14},{4,15},{5,16},{6,17},{7,18},{8,19},{9,... | collective-permute-start | bytes 1572872 | tf_op jit(solution)/shard_map/ppermute | solution.py:16
  60.5 51.5 %collective-permute-start.6 = (bf16[256,1024]{0,1:T(8,128)(2,1)S(1)}, bf16[256,1024]{0,1:T(8,128)(2,1)S(1)}, u32[]{:S(2)}, u32[]{:S(2)}) collective-permute-start(bf16[256,1024]{0,1:T(8,128)(2,1)S(1)} %bitcast.35), channel_id=1, source_target_pairs={{0,10},{1,11},{2,12},{3,13},{4,14},{5,15},{6,16},{7,17},{8,18},{9,... | collective-permute-start | bytes 1572872 | tf_op jit(solution)/shard_map/ppermute | solution.py:16
  67.1 56.2 %collective-permute-start.7 = (bf16[256,1024]{0,1:T(8,128)(2,1)S(1)}, bf16[256,1024]{0,1:T(8,128)(2,1)S(1)}, u32[]{:S(2)}, u32[]{:S(2)}) collective-permute-start(bf16[256,1024]{0,1:T(8,128)(2,1)S(1)} %bitcast.36), channel_id=1, source_target_pairs={{0,9},{1,10},{2,11},{3,12},{4,13},{5,14},{6,15},{7,16},{8,17},{9,1... | collective-permute-start | bytes 1572872 | tf_op jit(solution)/shard_map/ppermute | solution.py:16
  78.3 56.2 %collective-permute-start.8 = (bf16[256,1024]{0,1:T(8,128)(2,1)S(1)}, bf16[256,1024]{0,1:T(8,128)(2,1)S(1)}, u32[]{:S(2)}, u32[]{:S(2)}) collective-permute-start(bf16[256,1024]{0,1:T(8,128)(2,1)S(1)} %bitcast.37), channel_id=1, source_target_pairs={{0,8},{1,9},{2,10},{3,11},{4,12},{5,13},{6,14},{7,15},{8,16},{9,17... | collective-permute-start | bytes 1572872 | tf_op jit(solution)/shard_map/ppermute | solution.py:16
  89.5 51.6 %collective-permute-start.9 = (bf16[256,1024]{0,1:T(8,128)(2,1)S(1)}, bf16[256,1024]{0,1:T(8,128)(2,1)S(1)}, u32[]{:S(2)}, u32[]{:S(2)}) collective-permute-start(bf16[256,1024]{0,1:T(8,128)(2,1)S(1)} %bitcast.38), channel_id=1, source_target_pairs={{0,7},{1,8},{2,9},{3,10},{4,11},{5,12},{6,13},{7,14},{8,15},{9,16}... | collective-permute-start | bytes 1572872 | tf_op jit(solution)/shard_map/ppermute | solution.py:16
  100.8 48.1 %collective-permute-start.10 = (bf16[256,1024]{0,1:T(8,128)(2,1)S(1)}, bf16[256,1024]{0,1:T(8,128)(2,1)S(1)}, u32[]{:S(2)}, u32[]{:S(2)}) collective-permute-start(bf16[256,1024]{0,1:T(8,128)(2,1)S(1)} %bitcast.39), channel_id=1, source_target_pairs={{0,6},{1,7},{2,8},{3,9},{4,10},{5,11},{6,12},{7,13},{8,14},{9,15},... | collective-permute-start | bytes 1572872 | tf_op jit(solution)/shard_map/ppermute | solution.py:16
  112.0 50.1 %collective-permute-start.11 = (bf16[256,1024]{0,1:T(8,128)(2,1)S(1)}, bf16[256,1024]{0,1:T(8,128)(2,1)S(1)}, u32[]{:S(2)}, u32[]{:S(2)}) collective-permute-start(bf16[256,1024]{0,1:T(8,128)(2,1)S(1)} %bitcast.40), channel_id=1, source_target_pairs={{0,5},{1,6},{2,7},{3,8},{4,9},{5,10},{6,11},{7,12},{8,13},{9,14},{... | collective-permute-start | bytes 1572872 | tf_op jit(solution)/shard_map/ppermute | solution.py:16
  123.2 40.8 %collective-permute-start.12 = (bf16[256,1024]{0,1:T(8,128)(2,1)S(1)}, bf16[256,1024]{0,1:T(8,128)(2,1)S(1)}, u32[]{:S(2)}, u32[]{:S(2)}) collective-permute-start(bf16[256,1024]{0,1:T(8,128)(2,1)S(1)} %bitcast.41), channel_id=1, source_target_pairs={{0,4},{1,5},{2,6},{3,7},{4,8},{5,9},{6,10},{7,11},{8,12},{9,13},{1... | collective-permute-start | bytes 1572872 | tf_op jit(solution)/shard_map/ppermute | solution.py:16
  168.1 53.4 %collective-permute-start.20 = (bf16[256,1024]{0,1:T(8,128)(2,1)S(1)}, bf16[256,1024]{0,1:T(8,128)(2,1)S(1)}, u32[]{:S(2)}, u32[]{:S(2)}) collective-permute-start(bf16[256,1024]{0,1:T(8,128)(2,1)S(1)} %bitcast.49), channel_id=1, source_target_pairs={{5,0},{6,1},{7,2},{8,3},{9,4},{10,5},{11,6},{12,7},{13,8},{14,9},{... | collective-permute-start | bytes 1572872 | tf_op jit(solution)/shard_map/ppermute | solution.py:16
  175.7 57.1 %collective-permute-start.21 = (bf16[256,1024]{0,1:T(8,128)(2,1)S(1)}, bf16[256,1024]{0,1:T(8,128)(2,1)S(1)}, u32[]{:S(2)}, u32[]{:S(2)}) collective-permute-start(bf16[256,1024]{0,1:T(8,128)(2,1)S(1)} %bitcast.51), channel_id=1, source_target_pairs={{6,0},{7,1},{8,2},{9,3},{10,4},{11,5},{12,6},{13,7},{14,8},{15,9},... | collective-permute-start | bytes 1572872 | tf_op jit(solution)/shard_map/ppermute | solution.py:16
  180.9 81.3 %collective-permute-start.22 = (bf16[256,1024]{0,1:T(8,128)(2,1)S(1)}, bf16[256,1024]{0,1:T(8,128)(2,1)S(1)}, u32[]{:S(2)}, u32[]{:S(2)}) collective-permute-start(bf16[256,1024]{0,1:T(8,128)(2,1)S(1)} %bitcast.52), channel_id=1, source_target_pairs={{7,0},{8,1},{9,2},{10,3},{11,4},{12,5},{13,6},{14,7},{15,8},{16,9}... | collective-permute-start | bytes 1572872 | tf_op jit(solution)/shard_map/ppermute | solution.py:16
  194.8 70.5 %collective-permute-start.23 = (bf16[256,1024]{0,1:T(8,128)(2,1)S(1)}, bf16[256,1024]{0,1:T(8,128)(2,1)S(1)}, u32[]{:S(2)}, u32[]{:S(2)}) collective-permute-start(bf16[256,1024]{0,1:T(8,128)(2,1)S(1)} %bitcast.53), channel_id=1, source_target_pairs={{8,0},{9,1},{10,2},{11,3},{12,4},{13,5},{14,6},{15,7},{16,8},{17,9... | collective-permute-start | bytes 1572872 | tf_op jit(solution)/shard_map/ppermute | solution.py:16
  206.1 87.5 %collective-permute-start.24 = (bf16[256,1024]{0,1:T(8,128)(2,1)S(1)}, bf16[256,1024]{0,1:T(8,128)(2,1)S(1)}, u32[]{:S(2)}, u32[]{:S(2)}) collective-permute-start(bf16[256,1024]{0,1:T(8,128)(2,1)S(1)} %bitcast.54), channel_id=1, source_target_pairs={{9,0},{10,1},{11,2},{12,3},{13,4},{14,5},{15,6},{16,7},{17,8},{18,... | collective-permute-start | bytes 1572872 | tf_op jit(solution)/shard_map/ppermute | solution.py:16
  221.5 77.4 %collective-permute-start.25 = (bf16[256,1024]{0,1:T(8,128)(2,1)S(1)}, bf16[256,1024]{0,1:T(8,128)(2,1)S(1)}, u32[]{:S(2)}, u32[]{:S(2)}) collective-permute-start(bf16[256,1024]{0,1:T(8,128)(2,1)S(1)} %bitcast.55), channel_id=1, source_target_pairs={{10,0},{11,1},{12,2},{13,3},{14,4},{15,5},{16,6},{17,7},{18,8},{19... | collective-permute-start | bytes 1572872 | tf_op jit(solution)/shard_map/ppermute | solution.py:16
  232.8 76.5 %collective-permute-start.26 = (bf16[256,1024]{0,1:T(8,128)(2,1)S(1)}, bf16[256,1024]{0,1:T(8,128)(2,1)S(1)}, u32[]{:S(2)}, u32[]{:S(2)}) collective-permute-start(bf16[256,1024]{0,1:T(8,128)(2,1)S(1)} %bitcast.56), channel_id=1, source_target_pairs={{11,0},{12,1},{13,2},{14,3},{15,4},{16,5},{17,6},{18,7},{19,8},{20... | collective-permute-start | bytes 1572872 | tf_op jit(solution)/shard_map/ppermute | solution.py:16
  262.3 63.4 %collective-permute-start.27 = (bf16[256,1024]{0,1:T(8,128)(2,1)S(1)}, bf16[256,1024]{0,1:T(8,128)(2,1)S(1)}, u32[]{:S(2)}, u32[]{:S(2)}) collective-permute-start(bf16[256,1024]{0,1:T(8,128)(2,1)S(1)} %bitcast.57), channel_id=1, source_target_pairs={{12,0},{13,1},{14,2},{15,3},{16,4},{17,5},{18,6},{19,7},{20,8},{21... | collective-permute-start | bytes 1572872 | tf_op jit(solution)/shard_map/ppermute | solution.py:16
  265.3 69.4 %collective-permute-start.28 = (bf16[256,1024]{0,1:T(8,128)(2,1)S(1)}, bf16[256,1024]{0,1:T(8,128)(2,1)S(1)}, u32[]{:S(2)}, u32[]{:S(2)}) collective-permute-start(bf16[256,1024]{0,1:T(8,128)(2,1)S(1)} %bitcast.58), channel_id=1, source_target_pairs={{13,0},{14,1},{15,2},{16,3},{17,4},{18,5},{19,6},{20,7},{21,8},{22... | collective-permute-start | bytes 1572872 | tf_op jit(solution)/shard_map/ppermute | solution.py:16
  293.5 45.1 %collective-permute-start.29 = (bf16[256,1024]{0,1:T(8,128)(2,1)S(1)}, bf16[256,1024]{0,1:T(8,128)(2,1)S(1)}, u32[]{:S(2)}, u32[]{:S(2)}) collective-permute-start(bf16[256,1024]{0,1:T(8,128)(2,1)S(1)} %bitcast.59), channel_id=1, source_target_pairs={{14,0},{15,1},{16,2},{17,3},{18,4},{19,5},{20,6},{21,7},{22,8},{23... | collective-permute-start | bytes 1572872 | tf_op jit(solution)/shard_map/ppermute | solution.py:16
  299.0 75.2 %collective-permute-start.30 = (bf16[256,1024]{0,1:T(8,128)(2,1)S(1)}, bf16[256,1024]{0,1:T(8,128)(2,1)S(1)}, u32[]{:S(2)}, u32[]{:S(2)}) collective-permute-start(bf16[256,1024]{0,1:T(8,128)(2,1)S(1)} %bitcast.60), channel_id=1, source_target_pairs={{15,0},{16,1},{17,2},{18,3},{19,4},{20,5},{21,6},{22,7},{23,8},{24... | collective-permute-start | bytes 1572872 | tf_op jit(solution)/shard_map/ppermute | solution.py:16
  309.3 65.4 %collective-permute-start.31 = (bf16[256,1024]{0,1:T(8,128)(2,1)S(1)}, bf16[256,1024]{0,1:T(8,128)(2,1)S(1)}, u32[]{:S(2)}, u32[]{:S(2)}) collective-permute-start(bf16[256,1024]{0,1:T(8,128)(2,1)S(1)} %bitcast.61), channel_id=1, source_target_pairs={{16,0},{17,1},{18,2},{19,3},{20,4},{21,5},{22,6},{23,7},{24,8},{25... | collective-permute-start | bytes 1572872 | tf_op jit(solution)/shard_map/ppermute | solution.py:16
  395.6 227.6 %all-gather.9.cloned.1.call-start = ((), (), s32[]{:S(2)}) async-start(), calls=%async_computation.4 | async-start | bytes 21135360 | tf_op jit(solution)/shard_map/all_gather | solution.py:81
  537.0 198.7 %all-gather.11.cloned.1.call-start = ((), (), s32[]{:S(2)}) async-start(), calls=%async_computation.5 | async-start | bytes 21135360 | tf_op jit(solution)/shard_map/all_gather | solution.py:81
  (19 other events, 367.4 us)
Sparse Core Ops, SparseCore 0:
  395.8 115.0 all-gather.6
  537.1 86.1 all-gather.8
  649.6 86.1 all-gather.10
